TPU v7x, 256 devices: a whole 4x4x8 slice. The times are simulated.
256 devices in a mesh: seq: 64 (over x, z, core), ch: 4 (over y).
Axes of the slice: x: 4, y: 4, z: 8, core: 2. Of those that a mesh axis runs over, the one named last changes fastest.
Arguments:
- inputs: bfloat16 [8192, 4096], P('seq'), may hold values from -6 to 6
- norm_gain: float32 [4096], replicated, may hold values from 0.1 to 1.9
- in_weight: bfloat16 [4096, 3, 1024], P('seq', None, 'ch'), may hold values from -0.09375 to 0.09375
- short_filter: float32 [3, 3, 1024], P(None, None, 'ch'), may hold values from -4 to 4
- long_filter: float32 [8192, 1024], P('seq', 'ch'), may hold values from -2.2 to 2.2
- conv_bias: float32 [1024], P('ch'), may hold values from -4 to 4
- out_weight: bfloat16 [1024, 4096], P('ch', 'seq'), may hold values from -0.1875 to 0.1875
- out_grad: bfloat16 [8192, 4096], P('seq'), may hold values from -6 to 6
Outputs:
- block_out: bfloat16 [8192, 4096], P('seq', 'ch')
- in_grad: bfloat16 [8192, 4096], P('seq')
- filter_grad: float32 [8192, 1024], P('seq', 'ch')
All inputs are finite; a program needn't handle non-finite values.
Results may differ from a plain program's by a relative error of at most 0.013.
Values may be sent and summed in bfloat16 or wider, within the bound.
No kernel may reach another device: no remote copies, remote signals or barrier semaphores. Data moves between devices by JAX's collectives and lax.ppermute only.
A program may use at most 64 MiB of HBM per device.

v0:
```python
import math
import jax
import jax.numpy as jnp
from jax import lax
from jax.sharding import PartitionSpec as P

epsilon = 1e-05
highest = lax.Precision.HIGHEST


def passed_along(block, axis, distance):
    devices = range(lax.axis_size(axis))
    route = [(i - distance, i) for i in devices if i - distance in devices]
    return lax.ppermute(block, axis, route)


def regroup(data):
    return lax.all_to_all(data, "seq", split_axis=2, concat_axis=1, tiled=True)


def device_table(devices):
    first = jnp.arange(2 * devices, dtype=jnp.int32)[:, None]
    second = jnp.arange(devices, dtype=jnp.int32)[None, :]
    turns = first * second % (2 * devices)
    phases = 2.0 * math.pi / (2 * devices) * turns.astype(jnp.float32)
    return (jnp.cos(phases), jnp.sin(phases))


def phase_table(devices, place, local_rows, sign):
    total_len = 2 * devices * local_rows
    halves = jnp.arange(2, dtype=jnp.int32)[:, None, None]
    upper = jnp.arange(local_rows, dtype=jnp.int32)[None, :, None]
    lower = jnp.arange(local_rows, dtype=jnp.int32)[None, None, :]
    freqs = 2 * place + halves + 2 * devices * upper
    turns = freqs * lower % total_len
    phases = sign * 2.0 * math.pi / total_len * turns.astype(jnp.float32)
    return (jnp.cos(phases), jnp.sin(phases))


def to_spectrum(signals):
    count = signals.shape[0]
    local_rows = signals.shape[1]
    slab_width = signals.shape[2]
    devices = lax.axis_size("seq")
    place = lax.axis_index("seq")
    share = local_rows // devices
    spread = regroup(signals.reshape(count, 1, local_rows, slab_width))
    cos_dev, sin_dev = device_table(devices)
    real_part = jnp.einsum("kb,ubtc->utkc", cos_dev, spread, precision=highest)
    imag_part = -jnp.einsum("kb,ubtc->utkc", sin_dev, spread, precision=highest)
    joined = jnp.stack([real_part, imag_part], 1).reshape(count * 2, share, 2 * devices, slab_width)
    arrived = regroup(joined).reshape(count, 2, local_rows, 2, slab_width)
    cos_loc, sin_loc = phase_table(devices, place, local_rows, -1.0)
    zero_real = arrived[:, 0]
    zero_imag = arrived[:, 1]
    spec_real = jnp.einsum("ekt,utec->ukec", cos_loc, zero_real, precision=highest) - jnp.einsum(
        "ekt,utec->ukec", sin_loc, zero_imag, precision=highest
    )
    spec_imag = jnp.einsum("ekt,utec->ukec", sin_loc, zero_real, precision=highest) + jnp.einsum(
        "ekt,utec->ukec", cos_loc, zero_imag, precision=highest
    )
    return (spec_real, spec_imag)


def to_signal(spec_real, spec_imag):
    count = spec_real.shape[0]
    local_rows = spec_real.shape[1]
    slab_width = spec_real.shape[3]
    devices = lax.axis_size("seq")
    place = lax.axis_index("seq")
    share = local_rows // devices
    cos_loc, sin_loc = phase_table(devices, place, local_rows, 1.0)
    back_real = jnp.einsum("ekt,ukec->uetc", cos_loc, spec_real, precision=highest) - jnp.einsum(
        "ekt,ukec->uetc", sin_loc, spec_imag, precision=highest
    )
    back_imag = jnp.einsum("ekt,ukec->uetc", sin_loc, spec_real, precision=highest) + jnp.einsum(
        "ekt,ukec->uetc", cos_loc, spec_imag, precision=highest
    )
    joined = jnp.stack([back_real, back_imag], 1).reshape(count * 2, 2, local_rows, slab_width)
    arrived = regroup(joined).reshape(count, 2, 2 * devices, share, slab_width)
    cos_dev, sin_dev = device_table(devices)
    signal = jnp.einsum("kb,uktc->utbc", cos_dev, arrived[:, 0], precision=highest) - jnp.einsum(
        "kb,uktc->utbc", sin_dev, arrived[:, 1], precision=highest
    )
    returned = regroup(signal)
    return returned.reshape(count, local_rows, slab_width) / float(2 * devices * local_rows)


def per_device(
    inputs, norm_gain, in_weight, short_filter, long_filter, conv_bias, out_weight, out_grad
):
    local_rows = inputs.shape[0]
    model_width = inputs.shape[1]
    slab_width = long_filter.shape[1]
    taps = short_filter.shape[1]
    wide_inputs = inputs.astype(jnp.float32)
    inv_rms = lax.rsqrt(jnp.mean(wide_inputs * wide_inputs, axis=1, keepdims=True) + epsilon)
    normed = (wide_inputs * inv_rms * norm_gain).astype(jnp.bfloat16)
    in_panel, out_panel = (
        lax.all_gather(in_weight, "seq", axis=0, tiled=True),
        lax.all_gather(out_weight, "seq", axis=1, tiled=True),
    )
    in_flat = in_panel.reshape(model_width, 3 * slab_width)
    projected = jnp.dot(normed, in_flat, preferred_element_type=jnp.float32)
    projected = projected.astype(jnp.bfloat16).reshape(local_rows, 3, slab_width)
    upper_rim = passed_along(projected[local_rows - (taps - 1) :], "seq", 1)
    extended = jnp.concatenate([upper_rim, projected], 0).astype(jnp.float32)
    mixed = jnp.zeros((local_rows, 3, slab_width), jnp.float32)
    for offset in range(taps):
        begin = taps - 1 - offset
        mixed = mixed + short_filter[:, offset, :][None] * extended[begin : begin + local_rows]
    query_br = mixed[:, 0]
    key_br = mixed[:, 1]
    value_br = mixed[:, 2]
    product = key_br * value_br
    spec_real, spec_imag = to_spectrum(jnp.stack([product, long_filter]))
    sig_real, filt_real = (spec_real[0], spec_real[1])
    sig_imag, filt_imag = (spec_imag[0], spec_imag[1])
    conv_real = sig_real * filt_real - sig_imag * filt_imag
    conv_imag = sig_real * filt_imag + sig_imag * filt_real
    conv_out = to_signal(conv_real[None], conv_imag[None])[0]
    biased = conv_out + conv_bias * product
    gated = (query_br * biased).astype(jnp.bfloat16)
    partial_out = jnp.dot(gated, out_panel, preferred_element_type=jnp.float32)
    summed = lax.psum_scatter(
        partial_out.astype(jnp.bfloat16), "ch", scatter_dimension=1, tiled=True
    ).astype(jnp.float32)
    share = summed.shape[1]
    residual = lax.dynamic_slice_in_dim(wide_inputs, lax.axis_index("ch") * share, share, 1)
    block_out = (residual + summed).astype(jnp.bfloat16)
    gate_grad = jnp.dot(out_grad, out_panel.T, preferred_element_type=jnp.float32)
    carried = gate_grad * query_br
    all_real, all_imag = to_spectrum(jnp.stack([product, long_filter, carried]))
    sig_real, filt_real, grad_real = (all_real[0], all_real[1], all_real[2])
    sig_imag, filt_imag, grad_imag = (all_imag[0], all_imag[1], all_imag[2])
    back_real = grad_real * filt_real + grad_imag * filt_imag
    back_imag = grad_imag * filt_real - grad_real * filt_imag
    pair_real = grad_real * sig_real + grad_imag * sig_imag
    pair_imag = grad_imag * sig_real - grad_real * sig_imag
    returned = to_signal(jnp.stack([back_real, pair_real]), jnp.stack([back_imag, pair_imag]))
    back_conv = returned[0]
    filter_grad = returned[1] * float(local_rows * lax.axis_size("seq")) ** (-0.5)
    source_grad = back_conv + conv_bias * carried
    mixed_grad = jnp.stack([gate_grad * biased, source_grad * value_br, source_grad * key_br], 1)
    lower_rim = passed_along(mixed_grad[: taps - 1], "seq", -1)
    extended_back = jnp.concatenate([mixed_grad, lower_rim], 0)
    proj_grad = jnp.zeros((local_rows, 3, slab_width), jnp.float32)
    for offset in range(taps):
        proj_grad = (
            proj_grad
            + short_filter[:, offset, :][None] * extended_back[offset : offset + local_rows]
        )
    proj_grad = proj_grad.astype(jnp.bfloat16).reshape(local_rows, 3 * slab_width)
    partial_grad = jnp.dot(proj_grad, in_flat.T, preferred_element_type=jnp.float32)
    norm_grad = lax.psum(partial_grad, "ch")
    weighted = norm_grad * norm_gain
    inner_term = jnp.mean(weighted * wide_inputs, axis=1, keepdims=True)
    in_grad = (
        out_grad.astype(jnp.float32) + weighted * inv_rms - wide_inputs * inv_rms**3 * inner_term
    ).astype(jnp.bfloat16)
    return (block_out, in_grad, filter_grad)


def solution(mesh):
    return jax.shard_map(
        per_device,
        mesh=mesh,
        in_specs=(
            P("seq", None),
            P(),
            P("seq", None, "ch"),
            P(None, None, "ch"),
            P("seq", "ch"),
            P("ch"),
            P("ch", "seq"),
            P("seq", None),
        ),
        out_specs=(P("seq", "ch"), P("seq", None), P("seq", "ch")),
        check_vma=False,
    )
```

profile of v0, /device:TPU:1, one launch (start us, length us, event | category | flops | bytes accessed | tf_op | source)
XLA Modules:
  0.0 497.8 jit_solution(17033071886096602538)
XLA Ops:
  8.6 1.5 multiply_reduce_fusion.1
  11.6 83.9 %all-gather.3.cloned.1.call-done = bf16[4096,3,256]{2,0,1:T(8,128)(2,1)} async-done(((bf16[64,3,256]{2,0,1:T(8,128)(2,1)}), bf16[4096,3,256]{2,0,1:T(8,128)(2,1)}) %all-gather.3.cloned.1.call-update) | async-done | bytes 6291472 | tf_op jit(solution)/shard_map/all_gather | solution.py:100
  95.5 8.7 %copy.102 = bf16[4096,3,256]{0,2,1:T(8,128)(2,1)} copy(bf16[4096,3,256]{2,0,1:T(8,128)(2,1)} %all-gather.3.cloned.1.call-done) | data formatting | bytes 12582912 | tf_op jit(solution)/shard_map/all_gather | solution.py:100
  104.2 5.0 %convolution_convert_fusion.1 = bf16[128,768]{1,0:T(8,128)(2,1)S(1)} fusion(bf16[4096,768]{0,1:T(8,128)(2,1)} %bitcast.250, bf16[128,4096]{1,0:T(8,128)(2,1)S(1)} %copy-done, f32[4096]{0:T(1024)S(1)} %copy-done.13, f32[128]{0:T(128)S(1)} %get-tuple-element.27), kind=kOutput, calls=%fused_computation.25 | convolution fusion | flops 807501824 | bytes 7553536 | tf_op jit(solution)/shard_map/dot_general | solution.py:104
  109.2 2.9 collective-permute-start
  114.0 8.4 %all-to-all-start = ((f32[2,1,128,256]{3,0,1,2:T(2,128)}), f32[2,1,128,256]{3,0,1,2:T(2,128)S(1)}, u32[]{:S(2)}, u32[]{:S(2)}) async-start(f32[2,1,128,256]{3,0,1,2:T(2,128)} %copy.106), calls=%async_computation | async-start | bytes 524288 | tf_op jit(solution)/shard_map/all_to_all | solution.py:18
  122.4 50.2 %all-gather.5.cloned.1.call-done = bf16[256,4096]{0,1:T(8,128)(2,1)} async-done(((bf16[256,64]{0,1:T(8,128)(2,1)}), bf16[256,4096]{0,1:T(8,128)(2,1)}) %all-gather.5.cloned.1.call-update) | async-done | bytes 2097168 | tf_op jit(solution)/shard_map/all_gather | solution.py:101
  172.6 2.0 fusion.233
  175.3 1.1 copy.118
  176.5 6.8 %all-to-all-start.4 = ((f32[3,1,128,256]{3,1,0,2:T(1,128)}), f32[3,1,128,256]{3,1,0,2:T(1,128)}, u32[]{:S(2)}, u32[]{:S(2)}) async-start(f32[3,1,128,256]{3,1,0,2:T(1,128)} %copy.118), calls=%async_computation.5 | async-start | bytes 786432 | tf_op jit(solution)/shard_map/all_to_all | solution.py:18
  184.3 1.1 fusion.3
  185.8 1.8 copy.110
  187.6 10.2 %all-to-all-done.4 = f32[3,1,128,256]{3,1,0,2:T(1,128)} async-done(((f32[3,1,128,256]{3,1,0,2:T(1,128)}), f32[3,1,128,256]{3,1,0,2:T(1,128)}, u32[]{:S(2)}, u32[]{:S(2)}) %all-to-all-start.4) | async-done | bytes 393248 | tf_op jit(solution)/shard_map/all_to_all | solution.py:18
  197.7 20.1 %all-to-all-start.1 = ((f32[4,2,128,256]{3,1,0,2:T(2,128)}), f32[4,2,128,256]{3,1,0,2:T(2,128)}, u32[]{:S(2)}, u32[]{:S(2)}) async-start(f32[4,2,128,256]{3,1,0,2:T(2,128)} %copy.110), calls=%async_computation.1 | async-start | bytes 2097152 | tf_op jit(solution)/shard_map/all_to_all | solution.py:18
  217.8 1.1 copy.145
  219.0 1.5 convolution_bitcast_fusion.1
  220.5 1.5 fusion.2
  222.1 1.7 copy.122
  223.8 3.8 copy.123
  227.6 18.5 %all-to-all-done.1 = f32[4,2,128,256]{3,1,0,2:T(2,128)} async-done(((f32[4,2,128,256]{3,1,0,2:T(2,128)}), f32[4,2,128,256]{3,1,0,2:T(2,128)}, u32[]{:S(2)}, u32[]{:S(2)}) %all-to-all-start.1) | async-done | bytes 1048608 | tf_op jit(solution)/shard_map/all_to_all | solution.py:18
  246.1 6.2 %all-to-all-start.5 = ((f32[6,2,128,256]{3,1,0,2:T(2,128)}), f32[6,2,128,256]{3,1,0,2:T(2,128)S(1)}, u32[]{:S(2)}, u32[]{:S(2)}) async-start(f32[6,2,128,256]{3,1,0,2:T(2,128)} %copy.123), calls=%async_computation.6 | async-start | bytes 3145728 | tf_op jit(solution)/shard_map/all_to_all | solution.py:18
  252.4 1.8 copy.111
  254.1 1.4 fusion.231
  255.5 1.2 copy.146
  256.8 2.1 copy.147
  258.8 1.1 fusion.25
  260.0 1.1 fusion.23
  261.1 1.1 fusion.7
  262.3 1.1 fusion.6
  268.3 23.8 %all-to-all-done.5 = f32[6,2,128,256]{3,1,0,2:T(2,128)S(1)} async-done(((f32[6,2,128,256]{3,1,0,2:T(2,128)}), f32[6,2,128,256]{3,1,0,2:T(2,128)S(1)}, u32[]{:S(2)}, u32[]{:S(2)}) %all-to-all-start.5) | async-done | bytes 1572896 | tf_op jit(solution)/shard_map/all_to_all | solution.py:18
  292.0 6.3 %all-to-all-start.2 = ((f32[2,2,128,256]{3,1,0,2:T(2,128)}), f32[2,2,128,256]{3,1,0,2:T(2,128)}, u32[]{:S(2)}, u32[]{:S(2)}) async-start(f32[2,2,128,256]{3,1,0,2:T(2,128)} %copy.114), calls=%async_computation.2 | async-start | bytes 1048576 | tf_op jit(solution)/shard_map/all_to_all | solution.py:18
  299.1 1.4 fusion.229
  300.6 1.4 copy.148
  301.9 2.2 fusion.18
  304.1 2.2 fusion.16
  307.3 2.5 fusion.1
  309.9 1.3 fusion
  311.4 1.1 fusion.28
  312.5 1.1 fusion.5
  313.6 1.1 fusion.27
  314.8 1.1 fusion.4
  316.3 1.8 copy.128
  318.1 10.3 %all-to-all-start.6 = ((f32[4,2,128,256]{3,1,0,2:T(2,128)}), f32[4,2,128,256]{3,1,0,2:T(2,128)S(1)}, u32[]{:S(2)}, u32[]{:S(2)}) async-start(f32[4,2,128,256]{3,1,0,2:T(2,128)} %copy.128), calls=%async_computation.7 | async-start | bytes 2097152 | tf_op jit(solution)/shard_map/all_to_all | solution.py:18
  328.5 1.2 copy.116
  331.7 25.3 %all-to-all-done.6 = f32[4,2,128,256]{3,1,0,2:T(2,128)S(1)} async-done(((f32[4,2,128,256]{3,1,0,2:T(2,128)}), f32[4,2,128,256]{3,1,0,2:T(2,128)S(1)}, u32[]{:S(2)}, u32[]{:S(2)}) %all-to-all-start.6) | async-done | bytes 1048608 | tf_op jit(solution)/shard_map/all_to_all | solution.py:18
  357.0 6.8 %all-to-all-start.3 = ((f32[1,2,64,256]{3,1,0,2:T(2,128)}), f32[1,2,64,256]{3,1,0,2:T(2,128)}, u32[]{:S(2)}, u32[]{:S(2)}) async-start(f32[1,2,64,256]{3,1,0,2:T(2,128)} %copy.117), calls=%async_computation.3 | async-start | bytes 262144 | tf_op jit(solution)/shard_map/all_to_all | solution.py:18
  366.8 7.0 %all-to-all-done.3 = f32[1,2,64,256]{3,1,0,2:T(2,128)} async-done(((f32[1,2,64,256]{3,1,0,2:T(2,128)}), f32[1,2,64,256]{3,1,0,2:T(2,128)}, u32[]{:S(2)}, u32[]{:S(2)}) %all-to-all-start.3) | async-done | bytes 131104 | tf_op jit(solution)/shard_map/all_to_all | solution.py:18
  373.8 5.2 %all-to-all-start.7 = ((f32[2,2,64,256]{3,1,0,2:T(2,128)}), f32[2,2,64,256]{3,1,0,2:T(2,128)}, u32[]{:S(2)}, u32[]{:S(2)}) async-start(f32[2,2,64,256]{3,1,0,2:T(2,128)} %copy.132), calls=%async_computation.8 | async-start | bytes 524288 | tf_op jit(solution)/shard_map/all_to_all | solution.py:18
  379.0 1.6 multiply_bitcast_fusion.2
  380.6 1.6 div.33
  382.2 8.6 %all-to-all-done.7 = f32[2,2,64,256]{3,1,0,2:T(2,128)} async-done(((f32[2,2,64,256]{3,1,0,2:T(2,128)}), f32[2,2,64,256]{3,1,0,2:T(2,128)}, u32[]{:S(2)}, u32[]{:S(2)}) %all-to-all-start.7) | async-done | bytes 262176 | tf_op jit(solution)/shard_map/all_to_all | solution.py:18
  390.9 1.1 multiply_bitcast_fusion
  392.7 1.6 squeeze.53
  394.4 1.8 fusion.57
  396.2 1.8 convolution_convert_fusion
  400.0 2.4 collective-permute-start.1
  402.5 2.5 collective-permute-done.1
  405.0 6.5 %convolution_bitcast_fusion = f32[128,4096]{1,0:T(8,128)} fusion(bf16[4096,3,256]{2,0,1:T(8,128)(2,1)} %all-gather.3.cloned.1.call-done, f32[130,3,256]{2,0,1:T(8,128)S(1)} %pad_maximum_fusion.9, f32[3,256]{1,0:T(4,128)S(1)} %get-tuple-element.28, f32[3,256]{1,0:T(4,128)S(1)} %get-tuple-element.29, f32[3,256]{1,0:T(4,128)S(1)} %bitcast.267, ...), kind=kOutput, calls=%fused_computation | convolution fusion | flops 806092800 | bytes 9580544 | tf_op jit(solution)/shard_map/dot_general | solution.py:154
  411.6 1.6 convert_element_type.59
  413.9 5.8 %reduce-scatter.2.cloned.1.call-done = bf16[128,1024]{1,0:T(8,128)(2,1)} async-done(((bf16[128,4096]{1,0:T(8,128)(2,1)}), bf16[128,1024]{1,0:T(8,128)(2,1)}) %reduce-scatter.2.cloned.1.call-update) | async-done | bytes 262160 | tf_op jit(solution)/shard_map/reduce_scatter | solution.py:125
  419.7 1.9 add_convert_fusion
  421.6 65.2 %all-reduce.2.cloned.1.call-done = f32[128,4096]{1,0:T(8,128)} async-done(((f32[128,4096]{1,0:T(8,128)}), f32[128,4096]{1,0:T(8,128)}) %all-reduce.2.cloned.1.call-update) | async-done | bytes 2097168 | tf_op jit(solution)/shard_map/psum | solution.py:155
  486.9 2.1 multiply_reduce_fusion
  489.1 1.9 subtract_convert_fusion
  (98 shorter events, 22.8 us)
Async XLA Ops:
  7.2 88.3 %all-gather.3.cloned.1.call-start = ((), (), s32[]{:S(2)}) async-start(), calls=%async_computation.9 | async-start | bytes 6389760 | tf_op jit(solution)/shard_map/all_gather | solution.py:100
  7.9 164.7 %all-gather.5.cloned.1.call-start = ((), (), s32[]{:S(2)}) async-start(), calls=%async_computation.10 | async-start | bytes 2129920 | tf_op jit(solution)/shard_map/all_gather | solution.py:101
  10.7 93.5 %copy-start.17 = (f32[128]{0:T(128)}, f32[128]{0:T(128)S(1)}, u32[]{:S(2)}) copy-start(f32[128]{0:T(128)S(1)} %get-tuple-element.27) | copy-start | bytes 1540
  11.5 92.7 %copy-start = (bf16[128,4096]{1,0:T(8,128)(2,1)S(1)}, bf16[128,4096]{1,0:T(8,128)(2,1)}, u32[]{:S(2)}) copy-start(bf16[128,4096]{1,0:T(8,128)(2,1)} %param.8) | copy-start | bytes 3145732
  11.5 92.6 %copy-start.13 = (f32[4096]{0:T(1024)S(1)}, f32[4096]{0:T(1024)}, u32[]{:S(2)}) copy-start(f32[4096]{0:T(1024)} %param.9) | copy-start | bytes 49156
  109.2 3.8 copy-start.11
  109.2 3.6 collective-permute-start
  112.4 60.1 %copy-start.4 = (bf16[128,4096]{1,0:T(8,128)(2,1)S(1)}, bf16[128,4096]{1,0:T(8,128)(2,1)}, u32[]{:S(2)}) copy-start(bf16[128,4096]{1,0:T(8,128)(2,1)} %param.15) | copy-start | bytes 3145732
  114.0 61.3 %copy-start.12 = (f32[128,256]{1,0:T(8,128)S(1)}, f32[128,256]{1,0:T(8,128)}, u32[]{:S(2)}) copy-start(f32[128,256]{1,0:T(8,128)} %param.12) | copy-start | bytes 393220
  114.0 62.5 %all-to-all-start = ((f32[2,1,128,256]{3,0,1,2:T(2,128)}), f32[2,1,128,256]{3,0,1,2:T(2,128)S(1)}, u32[]{:S(2)}, u32[]{:S(2)}) async-start(f32[2,1,128,256]{3,0,1,2:T(2,128)} %copy.106), calls=%async_computation | async-start | bytes 524288 | tf_op jit(solution)/shard_map/all_to_all | solution.py:18
  174.6 0.6 copy-start.9
  176.5 21.3 %all-to-all-start.4 = ((f32[3,1,128,256]{3,1,0,2:T(1,128)}), f32[3,1,128,256]{3,1,0,2:T(1,128)}, u32[]{:S(2)}, u32[]{:S(2)}) async-start(f32[3,1,128,256]{3,1,0,2:T(1,128)} %copy.118), calls=%async_computation.5 | async-start | bytes 786432 | tf_op jit(solution)/shard_map/all_to_all | solution.py:18
  197.7 48.3 %all-to-all-start.1 = ((f32[4,2,128,256]{3,1,0,2:T(2,128)}), f32[4,2,128,256]{3,1,0,2:T(2,128)}, u32[]{:S(2)}, u32[]{:S(2)}) async-start(f32[4,2,128,256]{3,1,0,2:T(2,128)} %copy.110), calls=%async_computation.1 | async-start | bytes 2097152 | tf_op jit(solution)/shard_map/all_to_all | solution.py:18
  246.1 46.0 %all-to-all-start.5 = ((f32[6,2,128,256]{3,1,0,2:T(2,128)}), f32[6,2,128,256]{3,1,0,2:T(2,128)S(1)}, u32[]{:S(2)}, u32[]{:S(2)}) async-start(f32[6,2,128,256]{3,1,0,2:T(2,128)} %copy.123), calls=%async_computation.6 | async-start | bytes 3145728 | tf_op jit(solution)/shard_map/all_to_all | solution.py:18
  258.8 2.3 copy-start.3
  292.0 26.1 %all-to-all-start.2 = ((f32[2,2,128,256]{3,1,0,2:T(2,128)}), f32[2,2,128,256]{3,1,0,2:T(2,128)}, u32[]{:S(2)}, u32[]{:S(2)}) async-start(f32[2,2,128,256]{3,1,0,2:T(2,128)} %copy.114), calls=%async_computation.2 | async-start | bytes 1048576 | tf_op jit(solution)/shard_map/all_to_all | solution.py:18
  307.3 2.6 copy-start.6
  318.1 38.9 %all-to-all-start.6 = ((f32[4,2,128,256]{3,1,0,2:T(2,128)}), f32[4,2,128,256]{3,1,0,2:T(2,128)S(1)}, u32[]{:S(2)}, u32[]{:S(2)}) async-start(f32[4,2,128,256]{3,1,0,2:T(2,128)} %copy.128), calls=%async_computation.7 | async-start | bytes 2097152 | tf_op jit(solution)/shard_map/all_to_all | solution.py:18
  357.0 16.8 %all-to-all-start.3 = ((f32[1,2,64,256]{3,1,0,2:T(2,128)}), f32[1,2,64,256]{3,1,0,2:T(2,128)}, u32[]{:S(2)}, u32[]{:S(2)}) async-start(f32[1,2,64,256]{3,1,0,2:T(2,128)} %copy.117), calls=%async_computation.3 | async-start | bytes 262144 | tf_op jit(solution)/shard_map/all_to_all | solution.py:18
  365.3 29.1 %copy-start.15 = (f32[256]{0:T(256)S(1)}, f32[256]{0:T(256)}, u32[]{:S(2)}) copy-start(f32[256]{0:T(256)} %param.13) | copy-start | bytes 3076
  365.9 30.3 %copy-start.1 = (bf16[256,4096]{0,1:T(8,128)(2,1)S(1)}, bf16[256,4096]{0,1:T(8,128)(2,1)}, u32[]{:S(2)}) copy-start(bf16[256,4096]{0,1:T(8,128)(2,1)} %all-gather.5.cloned.1.call-done) | copy-start | bytes 6291460
  373.8 17.1 %all-to-all-start.7 = ((f32[2,2,64,256]{3,1,0,2:T(2,128)}), f32[2,2,64,256]{3,1,0,2:T(2,128)}, u32[]{:S(2)}, u32[]{:S(2)}) async-start(f32[2,2,64,256]{3,1,0,2:T(2,128)} %copy.132), calls=%async_computation.8 | async-start | bytes 524288 | tf_op jit(solution)/shard_map/all_to_all | solution.py:18
  378.9 40.8 %reduce-scatter.2.cloned.1.call-start = ((), (), s32[]{:S(2)}) async-start(), calls=%async_computation.11 | async-start | bytes 1310720 | tf_op jit(solution)/shard_map/reduce_scatter | solution.py:125
  398.0 7.0 %copy-start.7 = (f32[128,1,256]{2,0,1:T(8,128)S(1)}, f32[128,1,256]{2,0,1:T(8,128)}, u32[]{:S(2)}) copy-start(f32[128,1,256]{2,0,1:T(8,128)} %get-tuple-element.5) | copy-start | bytes 393220
  398.0 7.0 %copy-start.8 = (f32[128,1,256]{2,0,1:T(8,128)S(1)}, f32[128,1,256]{2,0,1:T(8,128)}, u32[]{:S(2)}) copy-start(f32[128,1,256]{2,0,1:T(8,128)} %get-tuple-element.19) | copy-start | bytes 393220
  398.0 88.9 %all-reduce.2.cloned.1.call-start = ((), (), s32[]{:S(2)}) async-start(), calls=%async_computation.12 | async-start | bytes 4194304 | tf_op jit(solution)/shard_map/psum | solution.py:155
  400.0 4.9 collective-permute-start.1
  411.6 1.6 copy-start.10
  411.6 75.3 %copy-start.14 = (f32[4096]{0:T(1024)S(1)}, f32[4096]{0:T(1024)}, u32[]{:S(2)}) copy-start(f32[4096]{0:T(1024)} %param.9) | copy-start | bytes 49156
  413.9 75.1 %copy-start.5 = (bf16[128,4096]{1,0:T(8,128)(2,1)S(1)}, bf16[128,4096]{1,0:T(8,128)(2,1)}, u32[]{:S(2)}) copy-start(bf16[128,4096]{1,0:T(8,128)(2,1)} %param.15) | copy-start | bytes 3145732
  413.9 75.1 %copy-start.16 = (f32[128]{0:T(128)S(1)}, f32[128]{0:T(128)}, u32[]{:S(2)}) copy-start(f32[128]{0:T(128)} %get-tuple-element.26) | copy-start | bytes 1540
  413.9 75.1 %copy-start.18 = (f32[128]{0:T(128)S(1)}, f32[128]{0:T(128)}, u32[]{:S(2)}) copy-start(f32[128]{0:T(128)} %copy-done.17) | copy-start | bytes 1540
  486.9 2.2 copy-start.2
Sparse Core Ops, SparseCore 0:
  10.8 84.6 all-gather.2
  98.3 74.2 all-gather.4
  398.1 21.5 reduce-scatter.1
  422.0 64.8 all-reduce.1
where the time goes:
time: 507 us; the launch traced here: 498 us
  waiting for transfers between devices  303 us (60%)
  starting transfers between devices  75.5 us (15%)
  local copies, waits for them, and re-layouts  43.7 us (9%)
  matrix products  43.5 us (9%)
  other arithmetic  17.6 us (3%)
  between operations  14.7 us (3%)
    all_to_all x8, waiting for transfers between devices, regroup(): return lax.all_to_all(data, 'seq', split_axis=2, concat_axis=1, tiled=True)  93.3 us
    all_gather x1, waiting for transfers between devices, per_device(): lax.all_gather(in_weight, 'seq', axis=0, tiled=True)  83.9 us
    all_to_all x8, starting transfers between devices, regroup(): return lax.all_to_all(data, 'seq', split_axis=2, concat_axis=1, tiled=True)  70 us
    psum x1, waiting for transfers between devices, per_device(): norm_grad = lax.psum(partial_grad, 'ch')  65.2 us
    all_gather x1, waiting for transfers between devices, per_device(): lax.all_gather(out_weight, 'seq', axis=1, tiled=True)  50.2 us
  transfers between devices with their start and end apart: 14, of which 12 were waited for; matrix products, arithmetic and copies ran while one was open for 19% of the time, Pallas kernels for 0%

commit v1 on v0

--- a/solution.py
+++ b/solution.py
@@ -152,7 +152,7 @@
         )
     proj_grad = proj_grad.astype(jnp.bfloat16).reshape(local_rows, 3 * slab_width)
     partial_grad = jnp.dot(proj_grad, in_flat.T, preferred_element_type=jnp.float32)
-    norm_grad = lax.psum(partial_grad, "ch")
+    norm_grad = jnp.sum(jax.lax.all_gather(partial_grad, "ch"), axis=0)
     weighted = norm_grad * norm_gain
     inner_term = jnp.mean(weighted * wide_inputs, axis=1, keepdims=True)
     in_grad = (

time: 507 us -> 531 us (1.047)
  waiting for transfers between devices: 303 us -> 325 us
    all_gather x0 -> x1, waiting for transfers between devices: none -> 86.7 us  [per_device(): norm_grad = jnp.sum(jax.lax.all_gather(partial_grad, 'ch'), axis=0)]
    psum x1 -> x0, waiting for transfers between devices: 65.2 us -> none  [per_device(): norm_grad = lax.psum(partial_grad, 'ch')]
  transfers between devices with their start and end apart: 14 -> 14, of which waited for: 12 -> 12; matrix products, arithmetic and copies ran while one was open for 19% -> 17% of each run, Pallas kernels for 0% -> 0%
where the time goes in v1:
time: 531 us; the launch traced here: 522 us
  waiting for transfers between devices  325 us (61%)
  starting transfers between devices  75.5 us (14%)
  local copies, waits for them, and re-layouts  45.1 us (8%)
  matrix products  43.5 us (8%)
  other arithmetic  18.5 us (3%)
  between operations  14.7 us (3%)
    all_to_all x8, waiting for transfers between devices, regroup(): return lax.all_to_all(data, 'seq', split_axis=2, concat_axis=1, tiled=True)  93.3 us
    all_gather x1, waiting for transfers between devices, per_device(): norm_grad = jnp.sum(jax.lax.all_gather(partial_grad, 'ch'), axis=0)  86.7 us
    all_gather x1, waiting for transfers between devices, per_device(): lax.all_gather(in_weight, 'seq', axis=0, tiled=True)  83.9 us
    all_to_all x8, starting transfers between devices, regroup(): return lax.all_to_all(data, 'seq', split_axis=2, concat_axis=1, tiled=True)  70 us
    all_gather x1, waiting for transfers between devices, per_device(): lax.all_gather(out_weight, 'seq', axis=1, tiled=True)  50.2 us
  transfers between devices with their start and end apart: 14, of which 12 were waited for; matrix products, arithmetic and copies ran while one was open for 17% of the time, Pallas kernels for 0%

profile of v1, /device:TPU:1, one launch (start us, length us, event | category | flops | bytes accessed | tf_op | source)
XLA Modules:
  0.0 522.2 jit_solution(1868952347212673070)
XLA Ops:
  8.6 1.5 multiply_reduce_fusion.1
  11.6 83.9 %all-gather.5.cloned.1.call-done = bf16[4096,3,256]{2,0,1:T(8,128)(2,1)} async-done(((bf16[64,3,256]{2,0,1:T(8,128)(2,1)}), bf16[4096,3,256]{2,0,1:T(8,128)(2,1)}) %all-gather.5.cloned.1.call-update) | async-done | bytes 6291472 | tf_op jit(solution)/shard_map/all_gather | solution.py:100
  95.5 8.7 %copy.102 = bf16[4096,3,256]{0,2,1:T(8,128)(2,1)} copy(bf16[4096,3,256]{2,0,1:T(8,128)(2,1)} %all-gather.5.cloned.1.call-done) | data formatting | bytes 12582912 | tf_op jit(solution)/shard_map/all_gather | solution.py:100
  104.2 5.0 convolution_convert_fusion.1
  109.2 2.9 collective-permute-start
  114.0 8.4 %all-to-all-start = ((f32[2,1,128,256]{3,0,1,2:T(2,128)}), f32[2,1,128,256]{3,0,1,2:T(2,128)S(1)}, u32[]{:S(2)}, u32[]{:S(2)}) async-start(f32[2,1,128,256]{3,0,1,2:T(2,128)} %copy.106), calls=%async_computation | async-start | bytes 524288 | tf_op jit(solution)/shard_map/all_to_all | solution.py:18
  122.4 50.2 %all-gather.7.cloned.1.call-done = bf16[256,4096]{0,1:T(8,128)(2,1)} async-done(((bf16[256,64]{0,1:T(8,128)(2,1)}), bf16[256,4096]{0,1:T(8,128)(2,1)}) %all-gather.7.cloned.1.call-update) | async-done | bytes 2097168 | tf_op jit(solution)/shard_map/all_gather | solution.py:101
  172.6 2.0 fusion.233
  175.3 1.2 copy.118
  176.5 6.8 %all-to-all-start.4 = ((f32[3,1,128,256]{3,1,0,2:T(1,128)}), f32[3,1,128,256]{3,1,0,2:T(1,128)}, u32[]{:S(2)}, u32[]{:S(2)}) async-start(f32[3,1,128,256]{3,1,0,2:T(1,128)} %copy.118), calls=%async_computation.5 | async-start | bytes 786432 | tf_op jit(solution)/shard_map/all_to_all | solution.py:18
  183.2 1.1 convolution_bitcast_fusion.2
  184.3 1.1 fusion.3
  185.8 1.8 copy.110
  187.6 10.2 %all-to-all-done.4 = f32[3,1,128,256]{3,1,0,2:T(1,128)} async-done(((f32[3,1,128,256]{3,1,0,2:T(1,128)}), f32[3,1,128,256]{3,1,0,2:T(1,128)}, u32[]{:S(2)}, u32[]{:S(2)}) %all-to-all-start.4) | async-done | bytes 393248 | tf_op jit(solution)/shard_map/all_to_all | solution.py:18
  197.7 20.1 %all-to-all-start.1 = ((f32[4,2,128,256]{3,1,0,2:T(2,128)}), f32[4,2,128,256]{3,1,0,2:T(2,128)}, u32[]{:S(2)}, u32[]{:S(2)}) async-start(f32[4,2,128,256]{3,1,0,2:T(2,128)} %copy.110), calls=%async_computation.1 | async-start | bytes 2097152 | tf_op jit(solution)/shard_map/all_to_all | solution.py:18
  217.8 1.1 copy.145
  219.0 1.5 convolution_bitcast_fusion.1
  220.5 1.5 fusion.2
  222.1 1.7 copy.122
  223.8 3.8 copy.123
  227.6 18.5 %all-to-all-done.1 = f32[4,2,128,256]{3,1,0,2:T(2,128)} async-done(((f32[4,2,128,256]{3,1,0,2:T(2,128)}), f32[4,2,128,256]{3,1,0,2:T(2,128)}, u32[]{:S(2)}, u32[]{:S(2)}) %all-to-all-start.1) | async-done | bytes 1048608 | tf_op jit(solution)/shard_map/all_to_all | solution.py:18
  246.1 6.2 %all-to-all-start.5 = ((f32[6,2,128,256]{3,1,0,2:T(2,128)}), f32[6,2,128,256]{3,1,0,2:T(2,128)S(1)}, u32[]{:S(2)}, u32[]{:S(2)}) async-start(f32[6,2,128,256]{3,1,0,2:T(2,128)} %copy.123), calls=%async_computation.6 | async-start | bytes 3145728 | tf_op jit(solution)/shard_map/all_to_all | solution.py:18
  252.4 1.8 copy.111
  254.2 1.4 fusion.231
  255.5 1.2 copy.146
  256.7 2.1 copy.147
  258.8 1.1 fusion.25
  259.9 1.1 fusion.23
  261.1 1.1 fusion.7
  262.2 1.1 fusion.6
  268.2 23.8 %all-to-all-done.5 = f32[6,2,128,256]{3,1,0,2:T(2,128)S(1)} async-done(((f32[6,2,128,256]{3,1,0,2:T(2,128)}), f32[6,2,128,256]{3,1,0,2:T(2,128)S(1)}, u32[]{:S(2)}, u32[]{:S(2)}) %all-to-all-start.5) | async-done | bytes 1572896 | tf_op jit(solution)/shard_map/all_to_all | solution.py:18
  292.0 6.3 %all-to-all-start.2 = ((f32[2,2,128,256]{3,1,0,2:T(2,128)}), f32[2,2,128,256]{3,1,0,2:T(2,128)}, u32[]{:S(2)}, u32[]{:S(2)}) async-start(f32[2,2,128,256]{3,1,0,2:T(2,128)} %copy.114), calls=%async_computation.2 | async-start | bytes 1048576 | tf_op jit(solution)/shard_map/all_to_all | solution.py:18
  299.2 1.4 fusion.229
  300.6 1.4 copy.148
  301.9 2.2 fusion.18
  304.2 2.2 fusion.16
  307.3 2.5 fusion.1
  309.9 1.3 fusion
  311.4 1.1 fusion.28
  312.5 1.1 fusion.5
  313.6 1.1 fusion.27
  314.8 1.1 fusion.4
  316.3 1.8 copy.128
  318.1 10.3 %all-to-all-start.6 = ((f32[4,2,128,256]{3,1,0,2:T(2,128)}), f32[4,2,128,256]{3,1,0,2:T(2,128)S(1)}, u32[]{:S(2)}, u32[]{:S(2)}) async-start(f32[4,2,128,256]{3,1,0,2:T(2,128)} %copy.128), calls=%async_computation.7 | async-start | bytes 2097152 | tf_op jit(solution)/shard_map/all_to_all | solution.py:18
  328.5 1.2 copy.116
  331.7 25.3 %all-to-all-done.6 = f32[4,2,128,256]{3,1,0,2:T(2,128)S(1)} async-done(((f32[4,2,128,256]{3,1,0,2:T(2,128)}), f32[4,2,128,256]{3,1,0,2:T(2,128)S(1)}, u32[]{:S(2)}, u32[]{:S(2)}) %all-to-all-start.6) | async-done | bytes 1048608 | tf_op jit(solution)/shard_map/all_to_all | solution.py:18
  357.0 6.8 %all-to-all-start.3 = ((f32[1,2,64,256]{3,1,0,2:T(2,128)}), f32[1,2,64,256]{3,1,0,2:T(2,128)}, u32[]{:S(2)}, u32[]{:S(2)}) async-start(f32[1,2,64,256]{3,1,0,2:T(2,128)} %copy.117), calls=%async_computation.3 | async-start | bytes 262144 | tf_op jit(solution)/shard_map/all_to_all | solution.py:18
  366.8 7.0 %all-to-all-done.3 = f32[1,2,64,256]{3,1,0,2:T(2,128)} async-done(((f32[1,2,64,256]{3,1,0,2:T(2,128)}), f32[1,2,64,256]{3,1,0,2:T(2,128)}, u32[]{:S(2)}, u32[]{:S(2)}) %all-to-all-start.3) | async-done | bytes 131104 | tf_op jit(solution)/shard_map/all_to_all | solution.py:18
  373.8 5.2 all-to-all-start.7
  379.0 1.6 multiply_bitcast_fusion.2
  380.6 1.7 div.33
  382.3 8.6 %all-to-all-done.7 = f32[2,2,64,256]{3,1,0,2:T(2,128)} async-done(((f32[2,2,64,256]{3,1,0,2:T(2,128)}), f32[2,2,64,256]{3,1,0,2:T(2,128)}, u32[]{:S(2)}, u32[]{:S(2)}) %all-to-all-start.7) | async-done | bytes 262176 | tf_op jit(solution)/shard_map/all_to_all | solution.py:18
  390.9 1.1 multiply_bitcast_fusion
  392.7 1.6 squeeze.53
  394.4 1.8 fusion.57
  396.2 1.8 convolution_convert_fusion
  400.0 2.4 collective-permute-start.1
  402.5 2.5 collective-permute-done.1
  405.0 6.5 %convolution_bitcast_fusion = f32[128,4096]{1,0:T(8,128)} fusion(bf16[4096,3,256]{2,0,1:T(8,128)(2,1)} %all-gather.5.cloned.1.call-done, f32[130,3,256]{2,0,1:T(8,128)S(1)} %pad_maximum_fusion.9, f32[3,256]{1,0:T(4,128)S(1)} %get-tuple-element.28, f32[3,256]{1,0:T(4,128)S(1)} %get-tuple-element.29, f32[3,256]{1,0:T(4,128)S(1)} %bitcast.269, ...), kind=kOutput, calls=%fused_computation | convolution fusion | flops 806092800 | bytes 9580544 | tf_op jit(solution)/shard_map/dot_general | solution.py:154
  413.2 6.6 %reduce-scatter.2.cloned.1.call-done = bf16[128,1024]{1,0:T(8,128)(2,1)} async-done(((bf16[128,4096]{1,0:T(8,128)(2,1)}), bf16[128,1024]{1,0:T(8,128)(2,1)}) %reduce-scatter.2.cloned.1.call-update) | async-done | bytes 262160 | tf_op jit(solution)/shard_map/reduce_scatter | solution.py:125
  419.7 1.7 add_convert_fusion
  421.5 86.7 %all-gather.9.cloned.1.call-done = f32[512,4096]{1,0:T(8,128)} async-done(((f32[128,4096]{1,0:T(8,128)}), f32[512,4096]{1,0:T(8,128)}) %all-gather.9.cloned.1.call-update) | async-done | bytes 8388624 | tf_op jit(solution)/shard_map/all_gather | solution.py:155
  508.2 4.2 reduce_sum.28
  513.6 1.9 subtract_convert_fusion
  (97 shorter events, 23.7 us)
Async XLA Ops:
  7.2 88.3 %all-gather.5.cloned.1.call-start = ((), (), s32[]{:S(2)}) async-start(), calls=%async_computation.9 | async-start | bytes 6389760 | tf_op jit(solution)/shard_map/all_gather | solution.py:100
  7.9 164.7 %all-gather.7.cloned.1.call-start = ((), (), s32[]{:S(2)}) async-start(), calls=%async_computation.10 | async-start | bytes 2129920 | tf_op jit(solution)/shard_map/all_gather | solution.py:101
  10.7 93.5 %copy-start.16 = (f32[128]{0:T(128)}, f32[128]{0:T(128)S(1)}, u32[]{:S(2)}) copy-start(f32[128]{0:T(128)S(1)} %get-tuple-element.27) | copy-start | bytes 1540
  11.6 92.6 %copy-start = (bf16[128,4096]{1,0:T(8,128)(2,1)S(1)}, bf16[128,4096]{1,0:T(8,128)(2,1)}, u32[]{:S(2)}) copy-start(bf16[128,4096]{1,0:T(8,128)(2,1)} %param.8) | copy-start | bytes 3145732
  11.6 92.6 %copy-start.12 = (f32[4096]{0:T(1024)S(1)}, f32[4096]{0:T(1024)}, u32[]{:S(2)}) copy-start(f32[4096]{0:T(1024)} %param.9) | copy-start | bytes 49156
  109.2 3.8 copy-start.10
  109.2 3.6 collective-permute-start
  112.4 60.1 %copy-start.3 = (bf16[128,4096]{1,0:T(8,128)(2,1)S(1)}, bf16[128,4096]{1,0:T(8,128)(2,1)}, u32[]{:S(2)}) copy-start(bf16[128,4096]{1,0:T(8,128)(2,1)} %param.15) | copy-start | bytes 3145732
  114.0 61.3 %copy-start.11 = (f32[128,256]{1,0:T(8,128)S(1)}, f32[128,256]{1,0:T(8,128)}, u32[]{:S(2)}) copy-start(f32[128,256]{1,0:T(8,128)} %param.12) | copy-start | bytes 393220
  114.0 62.5 %all-to-all-start = ((f32[2,1,128,256]{3,0,1,2:T(2,128)}), f32[2,1,128,256]{3,0,1,2:T(2,128)S(1)}, u32[]{:S(2)}, u32[]{:S(2)}) async-start(f32[2,1,128,256]{3,0,1,2:T(2,128)} %copy.106), calls=%async_computation | async-start | bytes 524288 | tf_op jit(solution)/shard_map/all_to_all | solution.py:18
  174.6 0.6 copy-start.8
  176.5 21.3 %all-to-all-start.4 = ((f32[3,1,128,256]{3,1,0,2:T(1,128)}), f32[3,1,128,256]{3,1,0,2:T(1,128)}, u32[]{:S(2)}, u32[]{:S(2)}) async-start(f32[3,1,128,256]{3,1,0,2:T(1,128)} %copy.118), calls=%async_computation.5 | async-start | bytes 786432 | tf_op jit(solution)/shard_map/all_to_all | solution.py:18
  197.7 48.3 %all-to-all-start.1 = ((f32[4,2,128,256]{3,1,0,2:T(2,128)}), f32[4,2,128,256]{3,1,0,2:T(2,128)}, u32[]{:S(2)}, u32[]{:S(2)}) async-start(f32[4,2,128,256]{3,1,0,2:T(2,128)} %copy.110), calls=%async_computation.1 | async-start | bytes 2097152 | tf_op jit(solution)/shard_map/all_to_all | solution.py:18
  246.1 46.0 %all-to-all-start.5 = ((f32[6,2,128,256]{3,1,0,2:T(2,128)}), f32[6,2,128,256]{3,1,0,2:T(2,128)S(1)}, u32[]{:S(2)}, u32[]{:S(2)}) async-start(f32[6,2,128,256]{3,1,0,2:T(2,128)} %copy.123), calls=%async_computation.6 | async-start | bytes 3145728 | tf_op jit(solution)/shard_map/all_to_all | solution.py:18
  258.8 2.3 copy-start.2
  292.0 26.1 %all-to-all-start.2 = ((f32[2,2,128,256]{3,1,0,2:T(2,128)}), f32[2,2,128,256]{3,1,0,2:T(2,128)}, u32[]{:S(2)}, u32[]{:S(2)}) async-start(f32[2,2,128,256]{3,1,0,2:T(2,128)} %copy.114), calls=%async_computation.2 | async-start | bytes 1048576 | tf_op jit(solution)/shard_map/all_to_all | solution.py:18
  307.3 2.6 copy-start.5
  318.1 38.9 %all-to-all-start.6 = ((f32[4,2,128,256]{3,1,0,2:T(2,128)}), f32[4,2,128,256]{3,1,0,2:T(2,128)S(1)}, u32[]{:S(2)}, u32[]{:S(2)}) async-start(f32[4,2,128,256]{3,1,0,2:T(2,128)} %copy.128), calls=%async_computation.7 | async-start | bytes 2097152 | tf_op jit(solution)/shard_map/all_to_all | solution.py:18
  357.0 16.8 %all-to-all-start.3 = ((f32[1,2,64,256]{3,1,0,2:T(2,128)}), f32[1,2,64,256]{3,1,0,2:T(2,128)}, u32[]{:S(2)}, u32[]{:S(2)}) async-start(f32[1,2,64,256]{3,1,0,2:T(2,128)} %copy.117), calls=%async_computation.3 | async-start | bytes 262144 | tf_op jit(solution)/shard_map/all_to_all | solution.py:18
  365.3 29.1 %copy-start.14 = (f32[256]{0:T(256)S(1)}, f32[256]{0:T(256)}, u32[]{:S(2)}) copy-start(f32[256]{0:T(256)} %param.13) | copy-start | bytes 3076
  365.9 30.3 %copy-start.1 = (bf16[256,4096]{0,1:T(8,128)(2,1)S(1)}, bf16[256,4096]{0,1:T(8,128)(2,1)}, u32[]{:S(2)}) copy-start(bf16[256,4096]{0,1:T(8,128)(2,1)} %all-gather.7.cloned.1.call-done) | copy-start | bytes 6291460
  373.8 17.1 %all-to-all-start.7 = ((f32[2,2,64,256]{3,1,0,2:T(2,128)}), f32[2,2,64,256]{3,1,0,2:T(2,128)}, u32[]{:S(2)}, u32[]{:S(2)}) async-start(f32[2,2,64,256]{3,1,0,2:T(2,128)} %copy.132), calls=%async_computation.8 | async-start | bytes 524288 | tf_op jit(solution)/shard_map/all_to_all | solution.py:18
  378.9 40.8 %reduce-scatter.2.cloned.1.call-start = ((), (), s32[]{:S(2)}) async-start(), calls=%async_computation.11 | async-start | bytes 1310720 | tf_op jit(solution)/shard_map/reduce_scatter | solution.py:125
  398.0 7.0 %copy-start.6 = (f32[128,1,256]{2,0,1:T(8,128)S(1)}, f32[128,1,256]{2,0,1:T(8,128)}, u32[]{:S(2)}) copy-start(f32[128,1,256]{2,0,1:T(8,128)} %get-tuple-element.5) | copy-start | bytes 393220
  398.0 7.0 %copy-start.7 = (f32[128,1,256]{2,0,1:T(8,128)S(1)}, f32[128,1,256]{2,0,1:T(8,128)}, u32[]{:S(2)}) copy-start(f32[128,1,256]{2,0,1:T(8,128)} %get-tuple-element.19) | copy-start | bytes 393220
  398.0 110.1 %all-gather.9.cloned.1.call-start = ((), (), s32[]{:S(2)}) async-start(), calls=%async_computation.12 | async-start | bytes 10485760 | tf_op jit(solution)/shard_map/all_gather | solution.py:155
  400.0 4.9 collective-permute-start.1
  411.5 0.9 copy-start.9
  508.2 4.2 copy-start.13
  512.4 1.2 copy-start.4
  512.4 1.2 copy-start.15
  512.4 1.2 copy-start.17
Sparse Core Ops, SparseCore 0:
  10.8 84.6 all-gather.4
  98.3 74.2 all-gather.6
  398.1 21.5 reduce-scatter.1
  421.4 86.7 all-gather.8
